TPU v7x, 32 devices: a whole 2x2x4 slice. The times are simulated.
32 devices in a mesh: seq: 16 (over z, y, core), mp: 2 (over x).
Axes of the slice: x: 2, y: 2, z: 4, core: 2. Of those that a mesh axis runs over, the one named last changes fastest.
Arguments:
- tokens: bfloat16 [4096, 2048], P('seq'), may hold values from -25 to 25
- lengths: int32 [32], replicated, may hold values from 1 to 1024, 4096 in all
- prefix_cache: bfloat16 [4, 2048, 512], P(None, 'seq'), may hold values from -1000 to 1000
- attn_gain: bfloat16 [2048], replicated, may hold values from 0.25 to 1.75
- w_query: bfloat16 [2048, 2048], P(None, 'mp'), may hold values from -0.25 to 0.25
- w_keyval: bfloat16 [2048, 512], replicated, may hold values from -0.125 to 0.125
- w_out: bfloat16 [2048, 2048], P('mp'), may hold values from -0.25 to 0.25
- final_gain: bfloat16 [2048], replicated, may hold values from 0.25 to 1.75
- w_head: bfloat16 [2048, 32000], P(None, ('seq', 'mp')), may hold values from -0.4375 to 0.4375
Outputs:
- hidden: bfloat16 [4096, 2048], P('seq', 'mp')
- suffix_cache: bfloat16 [4096, 512], P('seq')
- last_normed: bfloat16 [32, 2048], replicated
- greatest: float32 [32], replicated
Inputs may be any that keep to these rules, and one draw needn't show every extreme that they name: The lengths sum to 4096 and one of them equals 1024.
All inputs are finite; a program needn't handle non-finite values.
Results may differ from a plain program's by a relative error of at most 0.013.
Values may be sent and summed in bfloat16 or wider, within the bound.
No kernel may reach another device: no remote copies, remote signals or barrier semaphores. Data moves between devices by JAX's collectives and lax.ppermute only.
A program may use at most 64 MiB of HBM per device.

v0:
```python
import math
import jax
import jax.numpy as jnp
from jax import lax
from jax.sharding import PartitionSpec as P

QH = 32
KVH = 4
HD = 64
G = 4
RPG = 8
P_SIZE = 2048
epsilon = 1e-05


def passed_along(block, axis, distance):
    devices = range(lax.axis_size(axis))
    route = [((i - distance) % len(devices), i) for i in devices]
    return lax.ppermute(block, axis, route)


def rotate(source, places, head_count):
    half_dim = HD // 2
    row_count = source.shape[0]
    reshaped = source.reshape(row_count, head_count, HD)
    frequency = 10000.0 ** (-(jnp.arange(half_dim, dtype=jnp.float32) * 2.0 / HD))
    angles = places.astype(jnp.float32)[:, None] * frequency[None, :]
    cos_table = jnp.cos(angles)[:, None, :]
    sine_table = jnp.sin(angles)[:, None, :]
    leading = reshaped[..., :half_dim]
    second = reshaped[..., half_dim:]
    joined = jnp.concatenate(
        [leading * cos_table - second * sine_table, second * cos_table + leading * sine_table], -1
    )
    return joined.reshape(row_count, head_count * HD)


def attend(running, queries, kv_block, allowed):
    old_max, old_sum, numerator = running
    half_width = kv_block.shape[1] // 2
    kv_heads = queries.shape[1]
    key_rows = kv_block[:, :half_width].reshape(kv_block.shape[0], kv_heads, HD)
    val_rows = kv_block[:, half_width:].reshape(kv_block.shape[0], kv_heads, HD)
    scores = jnp.einsum("qgrd,ngd->grqn", queries, key_rows, preferred_element_type=jnp.float32) * (
        1.0 / math.sqrt(HD)
    )
    scores = jnp.where(allowed[None, None], scores, -jnp.inf)
    new_max = jnp.maximum(old_max, jnp.max(scores, -1))
    factor = jnp.exp(old_max - new_max)
    weights = jnp.exp(scores - new_max[..., None])
    new_sum = old_sum * factor + jnp.sum(weights, -1)
    numerator = numerator * factor[..., None] + jnp.einsum(
        "grqn,ngd->grqd", weights.astype(jnp.bfloat16), val_rows, preferred_element_type=jnp.float32
    )
    return (new_max, new_sum, numerator)


def suffix_allowed(source_dev, token_rows, request, position, request_end):
    key_place = source_dev * token_rows + jnp.arange(token_rows, dtype=jnp.int32)
    key_request = jnp.sum((key_place[:, None] >= request_end[None, :]).astype(jnp.int32), 1)
    return (
        (request[:, None] == key_request[None, :])
        & (key_place[None, :] <= position[:, None])
        & (source_dev >= 0)
    )


def prefix_allowed(group_of, row_count):
    key_group = (
        jnp.arange(G, dtype=jnp.int32)[:, None] + jnp.zeros((1, row_count), jnp.int32)
    ).reshape(-1)
    return group_of[:, None] == key_group[None, :]


def per_device(
    tokens, lengths, prefix_cache, attn_gain, w_query, w_keyval, w_out, final_gain, w_head
):
    token_rows = tokens.shape[0]
    model_width = tokens.shape[1]
    seq_devices = lax.axis_size("seq")
    seq_index = lax.axis_index("seq")
    mp_index = lax.axis_index("mp")
    part_width = model_width // lax.axis_size("mp")
    query_heads = w_query.shape[1] // HD
    group_size = QH // KVH
    kv_heads = max(1, query_heads // group_size)
    repeat_count = query_heads // kv_heads
    kv_first = mp_index * query_heads // group_size
    kv_width = KVH * HD
    request_count = lengths.shape[0]
    activations = tokens.astype(jnp.float32)
    normed = (
        activations
        * lax.rsqrt(jnp.mean(activations * activations, -1, keepdims=True) + epsilon)
        * attn_gain.astype(jnp.float32)
    ).astype(jnp.bfloat16)
    request_end = jnp.cumsum(lengths)
    starts = request_end - lengths
    position = seq_index * token_rows + jnp.arange(token_rows, dtype=jnp.int32)
    request = jnp.sum((position[:, None] >= request_end[None, :]).astype(jnp.int32), 1)
    request_table = request[:, None] == jnp.arange(request_count, dtype=jnp.int32)[None, :]
    offset = position - jnp.sum(jnp.where(request_table, starts[None, :], 0), 1)
    group_of = request // RPG
    query_full = jnp.dot(normed, w_query, preferred_element_type=jnp.float32)
    keyval = jnp.dot(normed, w_keyval, preferred_element_type=jnp.float32)
    queries = (
        rotate(query_full, P_SIZE + offset, query_heads)
        .astype(jnp.bfloat16)
        .reshape(token_rows, kv_heads, repeat_count, HD)
    )
    key_rows = rotate(keyval[:, :kv_width], P_SIZE + offset, KVH).astype(jnp.bfloat16)
    val_rows = keyval[:, kv_width:].astype(jnp.bfloat16)
    suffix_cache = jnp.concatenate([key_rows, val_rows], 1)
    own_suffix = jnp.concatenate(
        [
            lax.dynamic_slice_in_dim(key_rows, kv_first * HD, kv_heads * HD, 1),
            lax.dynamic_slice_in_dim(val_rows, kv_first * HD, kv_heads * HD, 1),
        ],
        1,
    )
    own_prefix = jnp.concatenate(
        [
            lax.dynamic_slice_in_dim(prefix_cache, kv_first * HD, kv_heads * HD, 2),
            lax.dynamic_slice_in_dim(prefix_cache, kv_width + kv_first * HD, kv_heads * HD, 2),
        ],
        2,
    )
    prefix_rows = own_prefix.shape[1]
    block_width = own_prefix.shape[2]
    running = (
        jnp.full((kv_heads, repeat_count, token_rows), -1e30, jnp.float32),
        jnp.zeros((kv_heads, repeat_count, token_rows), jnp.float32),
        jnp.zeros((kv_heads, repeat_count, token_rows, HD), jnp.float32),
    )
    prefix_mask = prefix_allowed(group_of, prefix_rows)
    running = attend(
        running, queries, own_prefix.reshape(G * prefix_rows, block_width), prefix_mask
    )
    running = attend(
        running,
        queries,
        own_suffix,
        suffix_allowed(seq_index, token_rows, request, position, request_end),
    )

    def cycle_hop(hop_count, loop_state):
        state_now, prefix_block, suffix_block = loop_state
        prefix_block, suffix_block = passed_along((prefix_block, suffix_block), "seq", 1)
        source_dev = (seq_index - hop_count) % seq_devices
        state_now = attend(
            state_now, queries, prefix_block.reshape(G * prefix_rows, block_width), prefix_mask
        )
        state_now = attend(
            state_now,
            queries,
            suffix_block,
            suffix_allowed(source_dev, token_rows, request, position, request_end),
        )
        return (state_now, prefix_block, suffix_block)

    running, unused_prefix, unused_suffix = lax.fori_loop(
        1, seq_devices, cycle_hop, (running, own_prefix, own_suffix)
    )
    final_max, final_sum, numerator = running
    context = numerator / final_sum[..., None]
    context = (
        jnp.transpose(context, (2, 0, 1, 3))
        .reshape(token_rows, query_heads * HD)
        .astype(jnp.bfloat16)
    )
    mixture = jnp.dot(context, w_out, preferred_element_type=jnp.float32)
    mixture = lax.psum_scatter(
        mixture.astype(jnp.bfloat16), "mp", scatter_dimension=1, tiled=True
    ).astype(jnp.float32)
    own_columns = lax.dynamic_slice_in_dim(activations, mp_index * part_width, part_width, 1)
    hidden = (own_columns + mixture).astype(jnp.bfloat16)
    local_last = request_end - 1 - seq_index * token_rows
    onehot = (local_last[:, None] == jnp.arange(token_rows, dtype=jnp.int32)[None, :]).astype(
        jnp.bfloat16
    )
    last_part = jnp.dot(onehot, hidden, preferred_element_type=jnp.float32)
    canvas = lax.dynamic_update_slice_in_dim(
        jnp.zeros((request_count, model_width), jnp.float32), last_part, mp_index * part_width, 1
    )
    last_rows = lax.psum(canvas, ("seq", "mp"))
    inv_rms = lax.rsqrt(jnp.mean(last_rows * last_rows, -1, keepdims=True) + epsilon)
    last_normed = (last_rows * final_gain.astype(jnp.float32) * inv_rms).astype(jnp.bfloat16)
    logits = jnp.dot(last_normed, w_head, preferred_element_type=jnp.float32)
    greatest = lax.pmax(jnp.max(logits, -1), ("seq", "mp"))
    return (hidden, suffix_cache, last_normed, greatest)


def solution(mesh):
    return jax.shard_map(
        per_device,
        mesh=mesh,
        in_specs=(
            P("seq", None),
            P(),
            P(None, "seq", None),
            P(),
            P(None, "mp"),
            P(),
            P("mp", None),
            P(),
            P(None, ("seq", "mp")),
        ),
        out_specs=(P("seq", "mp"), P("seq", None), P(), P()),
        check_vma=False,
    )
```

profile of v0, /device:TPU:0, one launch (start us, length us, event | category | flops | bytes accessed | tf_op | source)
XLA Modules:
  0.0 527.1 jit_solution(17378786312400722219)
XLA Ops:
  20.0 4.0 fusion.51
  33.5 2.3 fusion.47
  35.9 2.1 fusion.41
  38.0 280.5 %while.24 = (s32[]{:T(128)}, f32[2,8,256]{2,1,0:T(8,128)S(1)}, f32[2,8,256]{2,1,0:T(8,128)S(1)}, f32[2,8,256,64]{2,3,1,0:T(8,128)}, bf16[4,128,256]{1,0,2:T(4,12...) while((s32[]{:T(128)}, f32[2,8,256]{2,1,0:T(8,128)S(1)}, ...), condition=%wide.region_14.15_spmd.clone, body=%wide.region_8.14_spmd.clone.sunk | while | flops 841392384 | bytes 52473384 | solution.py:161
  38.5 2.6 collective-permute-start.1
  41.6 4.6 collective-permute-done
  53.3 2.1 fusion.113
  55.5 2.1 fusion.114
  58.2 6.6 %collective-permute-done = bf16[256,256]{0,1:T(8,128)(2,1)S(1)} collective-permute-done((bf16[256,256]{0,1:T(8,128)(2,1)S(1)}, bf16[256,256]{0,1:T(8,128)(2,1)S(1)}, u32[]{:S(2)}, u32[]{:S(2)}) %collective-permute-start) | collective-permute-done | bytes 131104 | tf_op jit(solution)/shard_map/while/body/eval_jaxpr/ppermute | solution.py:19
  72.0 2.1 fusion.113
  76.9 6.6 %collective-permute-done = bf16[256,256]{0,1:T(8,128)(2,1)S(1)} collective-permute-done((bf16[256,256]{0,1:T(8,128)(2,1)S(1)}, bf16[256,256]{0,1:T(8,128)(2,1)S(1)}, u32[]{:S(2)}, u32[]{:S(2)}) %collective-permute-start) | collective-permute-done | bytes 131104 | tf_op jit(solution)/shard_map/while/body/eval_jaxpr/ppermute | solution.py:19
  90.6 2.1 fusion.113
  92.7 2.1 fusion.114
  95.5 6.6 %collective-permute-done = bf16[256,256]{0,1:T(8,128)(2,1)S(1)} collective-permute-done((bf16[256,256]{0,1:T(8,128)(2,1)S(1)}, bf16[256,256]{0,1:T(8,128)(2,1)S(1)}, u32[]{:S(2)}, u32[]{:S(2)}) %collective-permute-start) | collective-permute-done | bytes 131104 | tf_op jit(solution)/shard_map/while/body/eval_jaxpr/ppermute | solution.py:19
  109.2 2.1 fusion.113
  114.1 6.6 %collective-permute-done = bf16[256,256]{0,1:T(8,128)(2,1)S(1)} collective-permute-done((bf16[256,256]{0,1:T(8,128)(2,1)S(1)}, bf16[256,256]{0,1:T(8,128)(2,1)S(1)}, u32[]{:S(2)}, u32[]{:S(2)}) %collective-permute-start) | collective-permute-done | bytes 131104 | tf_op jit(solution)/shard_map/while/body/eval_jaxpr/ppermute | solution.py:19
  127.9 2.1 fusion.113
  130.0 2.1 fusion.114
  132.8 6.6 %collective-permute-done = bf16[256,256]{0,1:T(8,128)(2,1)S(1)} collective-permute-done((bf16[256,256]{0,1:T(8,128)(2,1)S(1)}, bf16[256,256]{0,1:T(8,128)(2,1)S(1)}, u32[]{:S(2)}, u32[]{:S(2)}) %collective-permute-start) | collective-permute-done | bytes 131104 | tf_op jit(solution)/shard_map/while/body/eval_jaxpr/ppermute | solution.py:19
  146.5 2.1 fusion.113
  148.7 2.1 fusion.114
  151.4 6.6 %collective-permute-done = bf16[256,256]{0,1:T(8,128)(2,1)S(1)} collective-permute-done((bf16[256,256]{0,1:T(8,128)(2,1)S(1)}, bf16[256,256]{0,1:T(8,128)(2,1)S(1)}, u32[]{:S(2)}, u32[]{:S(2)}) %collective-permute-start) | collective-permute-done | bytes 131104 | tf_op jit(solution)/shard_map/while/body/eval_jaxpr/ppermute | solution.py:19
  165.2 2.1 fusion.113
  167.3 2.1 fusion.114
  170.0 6.6 %collective-permute-done = bf16[256,256]{0,1:T(8,128)(2,1)S(1)} collective-permute-done((bf16[256,256]{0,1:T(8,128)(2,1)S(1)}, bf16[256,256]{0,1:T(8,128)(2,1)S(1)}, u32[]{:S(2)}, u32[]{:S(2)}) %collective-permute-start) | collective-permute-done | bytes 131104 | tf_op jit(solution)/shard_map/while/body/eval_jaxpr/ppermute | solution.py:19
  183.8 2.1 fusion.113
  185.9 2.1 fusion.114
  188.7 6.6 %collective-permute-done = bf16[256,256]{0,1:T(8,128)(2,1)S(1)} collective-permute-done((bf16[256,256]{0,1:T(8,128)(2,1)S(1)}, bf16[256,256]{0,1:T(8,128)(2,1)S(1)}, u32[]{:S(2)}, u32[]{:S(2)}) %collective-permute-start) | collective-permute-done | bytes 131104 | tf_op jit(solution)/shard_map/while/body/eval_jaxpr/ppermute | solution.py:19
  202.4 2.1 fusion.113
  204.6 2.1 fusion.114
  207.3 6.6 %collective-permute-done = bf16[256,256]{0,1:T(8,128)(2,1)S(1)} collective-permute-done((bf16[256,256]{0,1:T(8,128)(2,1)S(1)}, bf16[256,256]{0,1:T(8,128)(2,1)S(1)}, u32[]{:S(2)}, u32[]{:S(2)}) %collective-permute-start) | collective-permute-done | bytes 131104 | tf_op jit(solution)/shard_map/while/body/eval_jaxpr/ppermute | solution.py:19
  221.1 2.1 fusion.113
  223.2 2.1 fusion.114
  225.9 6.6 %collective-permute-done = bf16[256,256]{0,1:T(8,128)(2,1)S(1)} collective-permute-done((bf16[256,256]{0,1:T(8,128)(2,1)S(1)}, bf16[256,256]{0,1:T(8,128)(2,1)S(1)}, u32[]{:S(2)}, u32[]{:S(2)}) %collective-permute-start) | collective-permute-done | bytes 131104 | tf_op jit(solution)/shard_map/while/body/eval_jaxpr/ppermute | solution.py:19
  239.7 2.1 fusion.113
  244.6 6.6 %collective-permute-done = bf16[256,256]{0,1:T(8,128)(2,1)S(1)} collective-permute-done((bf16[256,256]{0,1:T(8,128)(2,1)S(1)}, bf16[256,256]{0,1:T(8,128)(2,1)S(1)}, u32[]{:S(2)}, u32[]{:S(2)}) %collective-permute-start) | collective-permute-done | bytes 131104 | tf_op jit(solution)/shard_map/while/body/eval_jaxpr/ppermute | solution.py:19
  258.3 2.1 fusion.113
  263.2 6.6 %collective-permute-done = bf16[256,256]{0,1:T(8,128)(2,1)S(1)} collective-permute-done((bf16[256,256]{0,1:T(8,128)(2,1)S(1)}, bf16[256,256]{0,1:T(8,128)(2,1)S(1)}, u32[]{:S(2)}, u32[]{:S(2)}) %collective-permute-start) | collective-permute-done | bytes 131104 | tf_op jit(solution)/shard_map/while/body/eval_jaxpr/ppermute | solution.py:19
  277.0 2.1 fusion.113
  281.9 6.6 %collective-permute-done = bf16[256,256]{0,1:T(8,128)(2,1)S(1)} collective-permute-done((bf16[256,256]{0,1:T(8,128)(2,1)S(1)}, bf16[256,256]{0,1:T(8,128)(2,1)S(1)}, u32[]{:S(2)}, u32[]{:S(2)}) %collective-permute-start) | collective-permute-done | bytes 131104 | tf_op jit(solution)/shard_map/while/body/eval_jaxpr/ppermute | solution.py:19
  295.6 2.1 fusion.113
  300.5 6.6 %collective-permute-done = bf16[256,256]{0,1:T(8,128)(2,1)S(1)} collective-permute-done((bf16[256,256]{0,1:T(8,128)(2,1)S(1)}, bf16[256,256]{0,1:T(8,128)(2,1)S(1)}, u32[]{:S(2)}, u32[]{:S(2)}) %collective-permute-start) | collective-permute-done | bytes 131104 | tf_op jit(solution)/shard_map/while/body/eval_jaxpr/ppermute | solution.py:19
  314.2 2.1 fusion.113
  319.9 4.5 convolution_convert_fusion
  326.1 16.5 %reduce-scatter.2.cloned.1.call-done = bf16[256,1024]{1,0:T(8,128)(2,1)} async-done(((bf16[256,2048]{1,0:T(8,128)(2,1)}), bf16[256,1024]{1,0:T(8,128)(2,1)}) %reduce-scatter.2.cloned.1.call-update) | async-done | bytes 524304 | tf_op jit(solution)/shard_map/reduce_scatter | solution.py:172
  345.2 129.4 %all-reduce.2.cloned.1.call-done = f32[32,2048]{1,0:T(8,128)} async-done(((f32[32,2048]{1,0:T(8,128)}), f32[32,2048]{1,0:T(8,128)}) %all-reduce.2.cloned.1.call-update) | async-done | bytes 262160 | tf_op jit(solution)/shard_map/psum | solution.py:185
  476.7 3.6 convolution_reduce_fusion
  481.1 39.2 %pmax.7 = f32[32]{0:T(128)} all-reduce(f32[32]{0:T(128)S(1)} %convolution_reduce_fusion), channel_id=1, replica_groups=mesh['seq'=16,'mp'=2] {'seq','mp'}, use_global_device_ids=true, to_apply=%region_19.20 | all-reduce | flops 32 | bytes 256 | tf_op jit(solution)/shard_map/pmax | solution.py:189
  (459 shorter events, 160.4 us)
Async XLA Ops:
  7.2 6.3 %copy-start.33 = (s32[32]{0:T(128)S(1)}, s32[32]{0:T(128)}, u32[]{:S(2)}) copy-start(s32[32]{0:T(128)} %param.12) | copy-start | bytes 388
  7.2 335.4 %reduce-scatter.2.cloned.1.call-start = ((), (), s32[]{:S(2)}) async-start(), calls=%async_computation.1 | async-start | bytes 1572864 | tf_op jit(solution)/shard_map/reduce_scatter | solution.py:172
  10.0 10.0 %copy-start.1 = (bf16[256,2048]{1,0:T(8,128)(2,1)S(1)}, bf16[256,2048]{1,0:T(8,128)(2,1)}, u32[]{:S(2)}) copy-start(bf16[256,2048]{1,0:T(8,128)(2,1)} %param.11) | copy-start | bytes 3145732
  12.9 11.2 %copy-start.6 = (bf16[256,256]{1,0:T(8,128)(2,1)}, bf16[256,256]{1,0:T(8,128)(2,1)S(1)}, u32[]{:S(2)}) copy-start(bf16[256,256]{1,0:T(8,128)(2,1)S(1)} %slice.98) | copy-start | bytes 393220
  17.8 6.5 %copy-start.8 = (bf16[256,256]{1,0:T(8,128)(2,1)}, bf16[256,256]{1,0:T(8,128)(2,1)S(1)}, u32[]{:S(2)}) copy-start(bf16[256,256]{1,0:T(8,128)(2,1)S(1)} %copy.43) | copy-start | bytes 393220
  20.0 4.1 copy-start.14
  20.0 4.1 copy-start.16
  20.0 4.3 copy-start.21
  20.0 4.3 copy-start.30
  24.1 3.6 copy-start.23
  38.0 8.1 %collective-permute-start = (bf16[256,256]{0,1:T(8,128)(2,1)S(1)}, bf16[256,256]{0,1:T(8,128)(2,1)S(1)}, u32[]{:S(2)}, u32[]{:S(2)}) collective-permute-start(bf16[256,256]{0,1:T(8,128)(2,1)S(1)} %get-tuple-element.555), channel_id=1, source_target_pairs={{30,0},{0,2},{2,4},{4,6},{6,8},{8,10},{10,12},{12,14},{14,16},{16,... | collective-permute-start | bytes 393224 | tf_op jit(solution)/shard_map/while/body/eval_jaxpr/ppermute | solution.py:19
  38.5 10.4 %collective-permute-start.1 = (bf16[4,128,256]{1,0,2:T(4,128)(2,1)S(1)}, bf16[4,128,256]{1,0,2:T(4,128)(2,1)S(1)}, u32[]{:S(2)}, u32[]{:S(2)}) collective-permute-start(bf16[4,128,256]{1,0,2:T(4,128)(2,1)S(1)} %get-tuple-element.554), channel_id=1, source_target_pairs={{30,0},{0,2},{2,4},{4,6},{6,8},{8,10},{10,12},{12,14},{14,16},{16,... | collective-permute-start | bytes 786440 | tf_op jit(solution)/shard_map/while/body/eval_jaxpr/ppermute | solution.py:19
  57.7 7.1 %collective-permute-start = (bf16[256,256]{0,1:T(8,128)(2,1)S(1)}, bf16[256,256]{0,1:T(8,128)(2,1)S(1)}, u32[]{:S(2)}, u32[]{:S(2)}) collective-permute-start(bf16[256,256]{0,1:T(8,128)(2,1)S(1)} %get-tuple-element.555), channel_id=1, source_target_pairs={{30,0},{0,2},{2,4},{4,6},{6,8},{8,10},{10,12},{12,14},{14,16},{16,... | collective-permute-start | bytes 393224 | tf_op jit(solution)/shard_map/while/body/eval_jaxpr/ppermute | solution.py:19
  57.7 9.9 %collective-permute-start.1 = (bf16[4,128,256]{1,0,2:T(4,128)(2,1)S(1)}, bf16[4,128,256]{1,0,2:T(4,128)(2,1)S(1)}, u32[]{:S(2)}, u32[]{:S(2)}) collective-permute-start(bf16[4,128,256]{1,0,2:T(4,128)(2,1)S(1)} %get-tuple-element.554), channel_id=1, source_target_pairs={{30,0},{0,2},{2,4},{4,6},{6,8},{8,10},{10,12},{12,14},{14,16},{16,... | collective-permute-start | bytes 786440 | tf_op jit(solution)/shard_map/while/body/eval_jaxpr/ppermute | solution.py:19
  76.3 7.1 %collective-permute-start = (bf16[256,256]{0,1:T(8,128)(2,1)S(1)}, bf16[256,256]{0,1:T(8,128)(2,1)S(1)}, u32[]{:S(2)}, u32[]{:S(2)}) collective-permute-start(bf16[256,256]{0,1:T(8,128)(2,1)S(1)} %get-tuple-element.555), channel_id=1, source_target_pairs={{30,0},{0,2},{2,4},{4,6},{6,8},{8,10},{10,12},{12,14},{14,16},{16,... | collective-permute-start | bytes 393224 | tf_op jit(solution)/shard_map/while/body/eval_jaxpr/ppermute | solution.py:19
  76.4 9.9 %collective-permute-start.1 = (bf16[4,128,256]{1,0,2:T(4,128)(2,1)S(1)}, bf16[4,128,256]{1,0,2:T(4,128)(2,1)S(1)}, u32[]{:S(2)}, u32[]{:S(2)}) collective-permute-start(bf16[4,128,256]{1,0,2:T(4,128)(2,1)S(1)} %get-tuple-element.554), channel_id=1, source_target_pairs={{30,0},{0,2},{2,4},{4,6},{6,8},{8,10},{10,12},{12,14},{14,16},{16,... | collective-permute-start | bytes 786440 | tf_op jit(solution)/shard_map/while/body/eval_jaxpr/ppermute | solution.py:19
  94.9 7.1 %collective-permute-start = (bf16[256,256]{0,1:T(8,128)(2,1)S(1)}, bf16[256,256]{0,1:T(8,128)(2,1)S(1)}, u32[]{:S(2)}, u32[]{:S(2)}) collective-permute-start(bf16[256,256]{0,1:T(8,128)(2,1)S(1)} %get-tuple-element.555), channel_id=1, source_target_pairs={{30,0},{0,2},{2,4},{4,6},{6,8},{8,10},{10,12},{12,14},{14,16},{16,... | collective-permute-start | bytes 393224 | tf_op jit(solution)/shard_map/while/body/eval_jaxpr/ppermute | solution.py:19
  95.0 9.9 %collective-permute-start.1 = (bf16[4,128,256]{1,0,2:T(4,128)(2,1)S(1)}, bf16[4,128,256]{1,0,2:T(4,128)(2,1)S(1)}, u32[]{:S(2)}, u32[]{:S(2)}) collective-permute-start(bf16[4,128,256]{1,0,2:T(4,128)(2,1)S(1)} %get-tuple-element.554), channel_id=1, source_target_pairs={{30,0},{0,2},{2,4},{4,6},{6,8},{8,10},{10,12},{12,14},{14,16},{16,... | collective-permute-start | bytes 786440 | tf_op jit(solution)/shard_map/while/body/eval_jaxpr/ppermute | solution.py:19
  113.6 7.1 %collective-permute-start = (bf16[256,256]{0,1:T(8,128)(2,1)S(1)}, bf16[256,256]{0,1:T(8,128)(2,1)S(1)}, u32[]{:S(2)}, u32[]{:S(2)}) collective-permute-start(bf16[256,256]{0,1:T(8,128)(2,1)S(1)} %get-tuple-element.555), channel_id=1, source_target_pairs={{30,0},{0,2},{2,4},{4,6},{6,8},{8,10},{10,12},{12,14},{14,16},{16,... | collective-permute-start | bytes 393224 | tf_op jit(solution)/shard_map/while/body/eval_jaxpr/ppermute | solution.py:19
  113.6 9.9 %collective-permute-start.1 = (bf16[4,128,256]{1,0,2:T(4,128)(2,1)S(1)}, bf16[4,128,256]{1,0,2:T(4,128)(2,1)S(1)}, u32[]{:S(2)}, u32[]{:S(2)}) collective-permute-start(bf16[4,128,256]{1,0,2:T(4,128)(2,1)S(1)} %get-tuple-element.554), channel_id=1, source_target_pairs={{30,0},{0,2},{2,4},{4,6},{6,8},{8,10},{10,12},{12,14},{14,16},{16,... | collective-permute-start | bytes 786440 | tf_op jit(solution)/shard_map/while/body/eval_jaxpr/ppermute | solution.py:19
  132.2 7.1 %collective-permute-start = (bf16[256,256]{0,1:T(8,128)(2,1)S(1)}, bf16[256,256]{0,1:T(8,128)(2,1)S(1)}, u32[]{:S(2)}, u32[]{:S(2)}) collective-permute-start(bf16[256,256]{0,1:T(8,128)(2,1)S(1)} %get-tuple-element.555), channel_id=1, source_target_pairs={{30,0},{0,2},{2,4},{4,6},{6,8},{8,10},{10,12},{12,14},{14,16},{16,... | collective-permute-start | bytes 393224 | tf_op jit(solution)/shard_map/while/body/eval_jaxpr/ppermute | solution.py:19
  132.3 9.9 %collective-permute-start.1 = (bf16[4,128,256]{1,0,2:T(4,128)(2,1)S(1)}, bf16[4,128,256]{1,0,2:T(4,128)(2,1)S(1)}, u32[]{:S(2)}, u32[]{:S(2)}) collective-permute-start(bf16[4,128,256]{1,0,2:T(4,128)(2,1)S(1)} %get-tuple-element.554), channel_id=1, source_target_pairs={{30,0},{0,2},{2,4},{4,6},{6,8},{8,10},{10,12},{12,14},{14,16},{16,... | collective-permute-start | bytes 786440 | tf_op jit(solution)/shard_map/while/body/eval_jaxpr/ppermute | solution.py:19
  150.8 7.1 %collective-permute-start = (bf16[256,256]{0,1:T(8,128)(2,1)S(1)}, bf16[256,256]{0,1:T(8,128)(2,1)S(1)}, u32[]{:S(2)}, u32[]{:S(2)}) collective-permute-start(bf16[256,256]{0,1:T(8,128)(2,1)S(1)} %get-tuple-element.555), channel_id=1, source_target_pairs={{30,0},{0,2},{2,4},{4,6},{6,8},{8,10},{10,12},{12,14},{14,16},{16,... | collective-permute-start | bytes 393224 | tf_op jit(solution)/shard_map/while/body/eval_jaxpr/ppermute | solution.py:19
  150.9 9.9 %collective-permute-start.1 = (bf16[4,128,256]{1,0,2:T(4,128)(2,1)S(1)}, bf16[4,128,256]{1,0,2:T(4,128)(2,1)S(1)}, u32[]{:S(2)}, u32[]{:S(2)}) collective-permute-start(bf16[4,128,256]{1,0,2:T(4,128)(2,1)S(1)} %get-tuple-element.554), channel_id=1, source_target_pairs={{30,0},{0,2},{2,4},{4,6},{6,8},{8,10},{10,12},{12,14},{14,16},{16,... | collective-permute-start | bytes 786440 | tf_op jit(solution)/shard_map/while/body/eval_jaxpr/ppermute | solution.py:19
  169.5 7.1 %collective-permute-start = (bf16[256,256]{0,1:T(8,128)(2,1)S(1)}, bf16[256,256]{0,1:T(8,128)(2,1)S(1)}, u32[]{:S(2)}, u32[]{:S(2)}) collective-permute-start(bf16[256,256]{0,1:T(8,128)(2,1)S(1)} %get-tuple-element.555), channel_id=1, source_target_pairs={{30,0},{0,2},{2,4},{4,6},{6,8},{8,10},{10,12},{12,14},{14,16},{16,... | collective-permute-start | bytes 393224 | tf_op jit(solution)/shard_map/while/body/eval_jaxpr/ppermute | solution.py:19
  169.5 9.9 %collective-permute-start.1 = (bf16[4,128,256]{1,0,2:T(4,128)(2,1)S(1)}, bf16[4,128,256]{1,0,2:T(4,128)(2,1)S(1)}, u32[]{:S(2)}, u32[]{:S(2)}) collective-permute-start(bf16[4,128,256]{1,0,2:T(4,128)(2,1)S(1)} %get-tuple-element.554), channel_id=1, source_target_pairs={{30,0},{0,2},{2,4},{4,6},{6,8},{8,10},{10,12},{12,14},{14,16},{16,... | collective-permute-start | bytes 786440 | tf_op jit(solution)/shard_map/while/body/eval_jaxpr/ppermute | solution.py:19
  188.1 7.1 %collective-permute-start = (bf16[256,256]{0,1:T(8,128)(2,1)S(1)}, bf16[256,256]{0,1:T(8,128)(2,1)S(1)}, u32[]{:S(2)}, u32[]{:S(2)}) collective-permute-start(bf16[256,256]{0,1:T(8,128)(2,1)S(1)} %get-tuple-element.555), channel_id=1, source_target_pairs={{30,0},{0,2},{2,4},{4,6},{6,8},{8,10},{10,12},{12,14},{14,16},{16,... | collective-permute-start | bytes 393224 | tf_op jit(solution)/shard_map/while/body/eval_jaxpr/ppermute | solution.py:19
  188.2 9.9 %collective-permute-start.1 = (bf16[4,128,256]{1,0,2:T(4,128)(2,1)S(1)}, bf16[4,128,256]{1,0,2:T(4,128)(2,1)S(1)}, u32[]{:S(2)}, u32[]{:S(2)}) collective-permute-start(bf16[4,128,256]{1,0,2:T(4,128)(2,1)S(1)} %get-tuple-element.554), channel_id=1, source_target_pairs={{30,0},{0,2},{2,4},{4,6},{6,8},{8,10},{10,12},{12,14},{14,16},{16,... | collective-permute-start | bytes 786440 | tf_op jit(solution)/shard_map/while/body/eval_jaxpr/ppermute | solution.py:19
  206.7 7.1 %collective-permute-start = (bf16[256,256]{0,1:T(8,128)(2,1)S(1)}, bf16[256,256]{0,1:T(8,128)(2,1)S(1)}, u32[]{:S(2)}, u32[]{:S(2)}) collective-permute-start(bf16[256,256]{0,1:T(8,128)(2,1)S(1)} %get-tuple-element.555), channel_id=1, source_target_pairs={{30,0},{0,2},{2,4},{4,6},{6,8},{8,10},{10,12},{12,14},{14,16},{16,... | collective-permute-start | bytes 393224 | tf_op jit(solution)/shard_map/while/body/eval_jaxpr/ppermute | solution.py:19
  206.8 9.9 %collective-permute-start.1 = (bf16[4,128,256]{1,0,2:T(4,128)(2,1)S(1)}, bf16[4,128,256]{1,0,2:T(4,128)(2,1)S(1)}, u32[]{:S(2)}, u32[]{:S(2)}) collective-permute-start(bf16[4,128,256]{1,0,2:T(4,128)(2,1)S(1)} %get-tuple-element.554), channel_id=1, source_target_pairs={{30,0},{0,2},{2,4},{4,6},{6,8},{8,10},{10,12},{12,14},{14,16},{16,... | collective-permute-start | bytes 786440 | tf_op jit(solution)/shard_map/while/body/eval_jaxpr/ppermute | solution.py:19
  225.4 7.1 %collective-permute-start = (bf16[256,256]{0,1:T(8,128)(2,1)S(1)}, bf16[256,256]{0,1:T(8,128)(2,1)S(1)}, u32[]{:S(2)}, u32[]{:S(2)}) collective-permute-start(bf16[256,256]{0,1:T(8,128)(2,1)S(1)} %get-tuple-element.555), channel_id=1, source_target_pairs={{30,0},{0,2},{2,4},{4,6},{6,8},{8,10},{10,12},{12,14},{14,16},{16,... | collective-permute-start | bytes 393224 | tf_op jit(solution)/shard_map/while/body/eval_jaxpr/ppermute | solution.py:19
  225.4 9.9 %collective-permute-start.1 = (bf16[4,128,256]{1,0,2:T(4,128)(2,1)S(1)}, bf16[4,128,256]{1,0,2:T(4,128)(2,1)S(1)}, u32[]{:S(2)}, u32[]{:S(2)}) collective-permute-start(bf16[4,128,256]{1,0,2:T(4,128)(2,1)S(1)} %get-tuple-element.554), channel_id=1, source_target_pairs={{30,0},{0,2},{2,4},{4,6},{6,8},{8,10},{10,12},{12,14},{14,16},{16,... | collective-permute-start | bytes 786440 | tf_op jit(solution)/shard_map/while/body/eval_jaxpr/ppermute | solution.py:19
  244.0 7.1 %collective-permute-start = (bf16[256,256]{0,1:T(8,128)(2,1)S(1)}, bf16[256,256]{0,1:T(8,128)(2,1)S(1)}, u32[]{:S(2)}, u32[]{:S(2)}) collective-permute-start(bf16[256,256]{0,1:T(8,128)(2,1)S(1)} %get-tuple-element.555), channel_id=1, source_target_pairs={{30,0},{0,2},{2,4},{4,6},{6,8},{8,10},{10,12},{12,14},{14,16},{16,... | collective-permute-start | bytes 393224 | tf_op jit(solution)/shard_map/while/body/eval_jaxpr/ppermute | solution.py:19
  244.1 9.9 %collective-permute-start.1 = (bf16[4,128,256]{1,0,2:T(4,128)(2,1)S(1)}, bf16[4,128,256]{1,0,2:T(4,128)(2,1)S(1)}, u32[]{:S(2)}, u32[]{:S(2)}) collective-permute-start(bf16[4,128,256]{1,0,2:T(4,128)(2,1)S(1)} %get-tuple-element.554), channel_id=1, source_target_pairs={{30,0},{0,2},{2,4},{4,6},{6,8},{8,10},{10,12},{12,14},{14,16},{16,... | collective-permute-start | bytes 786440 | tf_op jit(solution)/shard_map/while/body/eval_jaxpr/ppermute | solution.py:19
  262.7 7.1 %collective-permute-start = (bf16[256,256]{0,1:T(8,128)(2,1)S(1)}, bf16[256,256]{0,1:T(8,128)(2,1)S(1)}, u32[]{:S(2)}, u32[]{:S(2)}) collective-permute-start(bf16[256,256]{0,1:T(8,128)(2,1)S(1)} %get-tuple-element.555), channel_id=1, source_target_pairs={{30,0},{0,2},{2,4},{4,6},{6,8},{8,10},{10,12},{12,14},{14,16},{16,... | collective-permute-start | bytes 393224 | tf_op jit(solution)/shard_map/while/body/eval_jaxpr/ppermute | solution.py:19
  262.7 9.9 %collective-permute-start.1 = (bf16[4,128,256]{1,0,2:T(4,128)(2,1)S(1)}, bf16[4,128,256]{1,0,2:T(4,128)(2,1)S(1)}, u32[]{:S(2)}, u32[]{:S(2)}) collective-permute-start(bf16[4,128,256]{1,0,2:T(4,128)(2,1)S(1)} %get-tuple-element.554), channel_id=1, source_target_pairs={{30,0},{0,2},{2,4},{4,6},{6,8},{8,10},{10,12},{12,14},{14,16},{16,... | collective-permute-start | bytes 786440 | tf_op jit(solution)/shard_map/while/body/eval_jaxpr/ppermute | solution.py:19
  281.3 7.1 %collective-permute-start = (bf16[256,256]{0,1:T(8,128)(2,1)S(1)}, bf16[256,256]{0,1:T(8,128)(2,1)S(1)}, u32[]{:S(2)}, u32[]{:S(2)}) collective-permute-start(bf16[256,256]{0,1:T(8,128)(2,1)S(1)} %get-tuple-element.555), channel_id=1, source_target_pairs={{30,0},{0,2},{2,4},{4,6},{6,8},{8,10},{10,12},{12,14},{14,16},{16,... | collective-permute-start | bytes 393224 | tf_op jit(solution)/shard_map/while/body/eval_jaxpr/ppermute | solution.py:19
  281.4 9.9 %collective-permute-start.1 = (bf16[4,128,256]{1,0,2:T(4,128)(2,1)S(1)}, bf16[4,128,256]{1,0,2:T(4,128)(2,1)S(1)}, u32[]{:S(2)}, u32[]{:S(2)}) collective-permute-start(bf16[4,128,256]{1,0,2:T(4,128)(2,1)S(1)} %get-tuple-element.554), channel_id=1, source_target_pairs={{30,0},{0,2},{2,4},{4,6},{6,8},{8,10},{10,12},{12,14},{14,16},{16,... | collective-permute-start | bytes 786440 | tf_op jit(solution)/shard_map/while/body/eval_jaxpr/ppermute | solution.py:19
  299.9 7.1 %collective-permute-start = (bf16[256,256]{0,1:T(8,128)(2,1)S(1)}, bf16[256,256]{0,1:T(8,128)(2,1)S(1)}, u32[]{:S(2)}, u32[]{:S(2)}) collective-permute-start(bf16[256,256]{0,1:T(8,128)(2,1)S(1)} %get-tuple-element.555), channel_id=1, source_target_pairs={{30,0},{0,2},{2,4},{4,6},{6,8},{8,10},{10,12},{12,14},{14,16},{16,... | collective-permute-start | bytes 393224 | tf_op jit(solution)/shard_map/while/body/eval_jaxpr/ppermute | solution.py:19
  300.0 9.9 %collective-permute-start.1 = (bf16[4,128,256]{1,0,2:T(4,128)(2,1)S(1)}, bf16[4,128,256]{1,0,2:T(4,128)(2,1)S(1)}, u32[]{:S(2)}, u32[]{:S(2)}) collective-permute-start(bf16[4,128,256]{1,0,2:T(4,128)(2,1)S(1)} %get-tuple-element.554), channel_id=1, source_target_pairs={{30,0},{0,2},{2,4},{4,6},{6,8},{8,10},{10,12},{12,14},{14,16},{16,... | collective-permute-start | bytes 786440 | tf_op jit(solution)/shard_map/while/body/eval_jaxpr/ppermute | solution.py:19
  319.9 4.6 copy-start.2
  324.4 19.7 %copy-start.32 = (s32[32]{0:T(128)S(1)}, s32[32]{0:T(128)}, u32[]{:S(2)}) copy-start(s32[32]{0:T(128)} %get-tuple-element.419) | copy-start | bytes 388
  324.4 20.7 %copy-start.31 = (bf16[2048]{0:T(1024)(128)(2,1)S(1)}, bf16[2048]{0:T(1024)(128)(2,1)}, u32[]{:S(2)}) copy-start(bf16[2048]{0:T(1024)(128)(2,1)} %param.18) | copy-start | bytes 12292
  324.5 150.1 %all-reduce.2.cloned.1.call-start = ((), (), s32[]{:S(2)}) async-start(), calls=%async_computation.2 | async-start | bytes 524288 | tf_op jit(solution)/shard_map/psum | solution.py:185
  326.1 154.2 %copy-start.7 = (bf16[256,256]{1,0:T(8,128)(2,1)S(1)}, bf16[256,256]{1,0:T(8,128)(2,1)}, u32[]{:S(2)}) copy-start(bf16[256,256]{1,0:T(8,128)(2,1)} %copy-done.6) | copy-start | bytes 393220
  326.1 154.2 %copy-start.9 = (bf16[256,256]{1,0:T(8,128)(2,1)S(1)}, bf16[256,256]{1,0:T(8,128)(2,1)}, u32[]{:S(2)}) copy-start(bf16[256,256]{1,0:T(8,128)(2,1)} %copy-done.8) | copy-start | bytes 393220
  344.1 176.1 %copy-start.4 = (bf16[256,1024]{1,0:T(8,128)(2,1)}, bf16[256,1024]{1,0:T(8,128)(2,1)S(1)}, u32[]{:S(2)}) copy-start(bf16[256,1024]{1,0:T(8,128)(2,1)S(1)} %add_convert_fusion) | copy-start | bytes 1572868
  476.7 43.5 %copy-start.11 = (bf16[32,2048]{1,0:T(8,128)(2,1)}, bf16[32,2048]{1,0:T(8,128)(2,1)S(1)}, u32[]{:S(2)}) copy-start(bf16[32,2048]{1,0:T(8,128)(2,1)S(1)} %multiply_convert_fusion.3) | copy-start | bytes 393220
  (32 other events, 49.0 us)
Sparse Core Ops, SparseCore 0:
  324.6 17.9 reduce-scatter.1
  349.6 124.9 all-reduce.1
where the time goes:
time: 528 us; the launch traced here: 527 us
  waiting for transfers between devices  272 us (52%)
  matrix products  117 us (22%)
  other arithmetic  60.6 us (11%)
  blocking collectives  39.2 us (7%)
  local copies, waits for them, and re-layouts  15.9 us (3%)
  between operations  14.7 us (3%)
    psum x1, waiting for transfers between devices, per_device(): last_rows = lax.psum(canvas, ('seq', 'mp'))  129 us
    ppermute x30, waiting for transfers between devices, passed_along(): return lax.ppermute(block, axis, route)  126 us
    dot_general x32, matrix products, attend(): jnp.einsum('grqn,ngd->grqd', weights.astype(jnp.bfloat16), val_rows, pref...  67.5 us
    reduce_sum x32, other arithmetic, attend(): new_sum = old_sum * factor + jnp.sum(weights, -1)  40.8 us
    pmax x1, blocking collectives, per_device(): greatest = lax.pmax(jnp.max(logits, -1), ('seq', 'mp'))  39.2 us
    dot_general x32, matrix products, attend(): jnp.einsum('qgrd,ngd->grqn', queries, key_rows, preferred_element_type=jn...  35.1 us
    reduce_scatter x1, waiting for transfers between devices, per_device(): lax.psum_scatter(mixture.astype(jnp.bfloat16), 'mp', scatter_dimension=1,...  16.5 us
  transfers between devices with their start and end apart: 32, of which 32 were waited for; matrix products, arithmetic and copies ran while one was open for 4% of the time, Pallas kernels for 0%

commit v1 on v0

--- a/solution.py
+++ b/solution.py
@@ -182,7 +182,7 @@
     canvas = lax.dynamic_update_slice_in_dim(
         jnp.zeros((request_count, model_width), jnp.float32), last_part, mp_index * part_width, 1
     )
-    last_rows = lax.psum(canvas, ("seq", "mp"))
+    last_rows = jnp.sum(lax.all_gather(canvas, ("seq", "mp")), axis=0)
     inv_rms = lax.rsqrt(jnp.mean(last_rows * last_rows, -1, keepdims=True) + epsilon)
     last_normed = (last_rows * final_gain.astype(jnp.float32) * inv_rms).astype(jnp.bfloat16)
     logits = jnp.dot(last_normed, w_head, preferred_element_type=jnp.float32)

time: 528 us -> 482 us (0.913)
  waiting for transfers between devices: 272 us -> 222 us
    psum x1 -> x0, waiting for transfers between devices: 129 us -> none  [per_device(): last_rows = lax.psum(canvas, ('seq', 'mp'))]
    all_gather x0 -> x1, waiting for transfers between devices: none -> 78.9 us  [per_device(): last_rows = jnp.sum(lax.all_gather(canvas, ('seq', 'mp')), axis=0)]
where the time goes in v1:
time: 482 us; the launch traced here: 481 us
  waiting for transfers between devices  222 us (46%)
  matrix products  117 us (24%)
  other arithmetic  65 us (13%)
  blocking collectives  39.2 us (8%)
  local copies, waits for them, and re-layouts  15.9 us (3%)
  between operations  14.6 us (3%)
  starting transfers between devices  5.05 us (1%)
    ppermute x30, waiting for transfers between devices, passed_along(): return lax.ppermute(block, axis, route)  126 us
    all_gather x1, waiting for transfers between devices, per_device(): last_rows = jnp.sum(lax.all_gather(canvas, ('seq', 'mp')), axis=0)  78.9 us
    dot_general x32, matrix products, attend(): jnp.einsum('grqn,ngd->grqd', weights.astype(jnp.bfloat16), val_rows, pref...  67.8 us
    reduce_sum x32, other arithmetic, attend(): new_sum = old_sum * factor + jnp.sum(weights, -1)  40.8 us
    pmax x1, blocking collectives, per_device(): greatest = lax.pmax(jnp.max(logits, -1), ('seq', 'mp'))  39.2 us
    dot_general x32, matrix products, attend(): jnp.einsum('qgrd,ngd->grqn', queries, key_rows, preferred_element_type=jn...  35 us
    reduce_scatter x1, waiting for transfers between devices, per_device(): lax.psum_scatter(mixture.astype(jnp.bfloat16), 'mp', scatter_dimension=1,...  16.3 us
  transfers between devices with their start and end apart: 32, of which 32 were waited for; matrix products, arithmetic and copies ran while one was open for 4% of the time, Pallas kernels for 0%

profile of v1, /device:TPU:0, one launch (start us, length us, event | category | flops | bytes accessed | tf_op | source)
XLA Modules:
  0.0 481.1 jit_solution(15878601705479982073)
XLA Ops:
  20.2 4.0 fusion.52
  35.9 2.3 fusion.47
  38.2 2.1 fusion.41
  40.4 280.8 %while.24 = (s32[]{:T(128)}, f32[2,8,256]{2,1,0:T(8,128)S(1)}, f32[2,8,256]{2,1,0:T(8,128)S(1)}, f32[2,8,256,64]{2,3,1,0:T(8,128)}, bf16[4,128,256]{1,0,2:T(4,12...) while((s32[]{:T(128)}, f32[2,8,256]{2,1,0:T(8,128)S(1)}, ...), condition=%wide.region_14.15_spmd.clone, body=%wide.region_8.14_spmd.clone.sunk | while | flops 841392384 | bytes 52473384 | solution.py:161
  40.9 2.6 collective-permute-start.1
  43.9 4.6 collective-permute-done
  55.7 2.1 fusion.114
  57.8 2.1 fusion.115
  60.6 6.6 %collective-permute-done = bf16[256,256]{0,1:T(8,128)(2,1)S(1)} collective-permute-done((bf16[256,256]{0,1:T(8,128)(2,1)S(1)}, bf16[256,256]{0,1:T(8,128)(2,1)S(1)}, u32[]{:S(2)}, u32[]{:S(2)}) %collective-permute-start) | collective-permute-done | bytes 131104 | tf_op jit(solution)/shard_map/while/body/eval_jaxpr/ppermute | solution.py:19
  74.3 2.1 fusion.114
  76.5 2.1 fusion.115
  79.2 6.6 %collective-permute-done = bf16[256,256]{0,1:T(8,128)(2,1)S(1)} collective-permute-done((bf16[256,256]{0,1:T(8,128)(2,1)S(1)}, bf16[256,256]{0,1:T(8,128)(2,1)S(1)}, u32[]{:S(2)}, u32[]{:S(2)}) %collective-permute-start) | collective-permute-done | bytes 131104 | tf_op jit(solution)/shard_map/while/body/eval_jaxpr/ppermute | solution.py:19
  93.0 2.1 fusion.114
  95.1 2.1 fusion.115
  97.9 6.6 %collective-permute-done = bf16[256,256]{0,1:T(8,128)(2,1)S(1)} collective-permute-done((bf16[256,256]{0,1:T(8,128)(2,1)S(1)}, bf16[256,256]{0,1:T(8,128)(2,1)S(1)}, u32[]{:S(2)}, u32[]{:S(2)}) %collective-permute-start) | collective-permute-done | bytes 131104 | tf_op jit(solution)/shard_map/while/body/eval_jaxpr/ppermute | solution.py:19
  111.6 2.1 fusion.114
  113.8 2.1 fusion.115
  116.6 6.6 %collective-permute-done = bf16[256,256]{0,1:T(8,128)(2,1)S(1)} collective-permute-done((bf16[256,256]{0,1:T(8,128)(2,1)S(1)}, bf16[256,256]{0,1:T(8,128)(2,1)S(1)}, u32[]{:S(2)}, u32[]{:S(2)}) %collective-permute-start) | collective-permute-done | bytes 131104 | tf_op jit(solution)/shard_map/while/body/eval_jaxpr/ppermute | solution.py:19
  130.3 2.1 fusion.114
  132.4 2.1 fusion.115
  135.2 6.6 %collective-permute-done = bf16[256,256]{0,1:T(8,128)(2,1)S(1)} collective-permute-done((bf16[256,256]{0,1:T(8,128)(2,1)S(1)}, bf16[256,256]{0,1:T(8,128)(2,1)S(1)}, u32[]{:S(2)}, u32[]{:S(2)}) %collective-permute-start) | collective-permute-done | bytes 131104 | tf_op jit(solution)/shard_map/while/body/eval_jaxpr/ppermute | solution.py:19
  148.9 2.1 fusion.114
  151.1 2.1 fusion.115
  153.9 6.6 %collective-permute-done = bf16[256,256]{0,1:T(8,128)(2,1)S(1)} collective-permute-done((bf16[256,256]{0,1:T(8,128)(2,1)S(1)}, bf16[256,256]{0,1:T(8,128)(2,1)S(1)}, u32[]{:S(2)}, u32[]{:S(2)}) %collective-permute-start) | collective-permute-done | bytes 131104 | tf_op jit(solution)/shard_map/while/body/eval_jaxpr/ppermute | solution.py:19
  167.6 2.1 fusion.114
  172.5 6.6 %collective-permute-done = bf16[256,256]{0,1:T(8,128)(2,1)S(1)} collective-permute-done((bf16[256,256]{0,1:T(8,128)(2,1)S(1)}, bf16[256,256]{0,1:T(8,128)(2,1)S(1)}, u32[]{:S(2)}, u32[]{:S(2)}) %collective-permute-start) | collective-permute-done | bytes 131104 | tf_op jit(solution)/shard_map/while/body/eval_jaxpr/ppermute | solution.py:19
  186.3 2.1 fusion.114
  191.2 6.6 %collective-permute-done = bf16[256,256]{0,1:T(8,128)(2,1)S(1)} collective-permute-done((bf16[256,256]{0,1:T(8,128)(2,1)S(1)}, bf16[256,256]{0,1:T(8,128)(2,1)S(1)}, u32[]{:S(2)}, u32[]{:S(2)}) %collective-permute-start) | collective-permute-done | bytes 131104 | tf_op jit(solution)/shard_map/while/body/eval_jaxpr/ppermute | solution.py:19
  204.9 2.1 fusion.114
  209.8 6.6 %collective-permute-done = bf16[256,256]{0,1:T(8,128)(2,1)S(1)} collective-permute-done((bf16[256,256]{0,1:T(8,128)(2,1)S(1)}, bf16[256,256]{0,1:T(8,128)(2,1)S(1)}, u32[]{:S(2)}, u32[]{:S(2)}) %collective-permute-start) | collective-permute-done | bytes 131104 | tf_op jit(solution)/shard_map/while/body/eval_jaxpr/ppermute | solution.py:19
  223.6 2.1 fusion.114
  228.5 6.6 %collective-permute-done = bf16[256,256]{0,1:T(8,128)(2,1)S(1)} collective-permute-done((bf16[256,256]{0,1:T(8,128)(2,1)S(1)}, bf16[256,256]{0,1:T(8,128)(2,1)S(1)}, u32[]{:S(2)}, u32[]{:S(2)}) %collective-permute-start) | collective-permute-done | bytes 131104 | tf_op jit(solution)/shard_map/while/body/eval_jaxpr/ppermute | solution.py:19
  242.2 2.1 fusion.114
  247.1 6.6 %collective-permute-done = bf16[256,256]{0,1:T(8,128)(2,1)S(1)} collective-permute-done((bf16[256,256]{0,1:T(8,128)(2,1)S(1)}, bf16[256,256]{0,1:T(8,128)(2,1)S(1)}, u32[]{:S(2)}, u32[]{:S(2)}) %collective-permute-start) | collective-permute-done | bytes 131104 | tf_op jit(solution)/shard_map/while/body/eval_jaxpr/ppermute | solution.py:19
  260.9 2.1 fusion.114
  263.0 2.1 fusion.115
  265.8 6.6 %collective-permute-done = bf16[256,256]{0,1:T(8,128)(2,1)S(1)} collective-permute-done((bf16[256,256]{0,1:T(8,128)(2,1)S(1)}, bf16[256,256]{0,1:T(8,128)(2,1)S(1)}, u32[]{:S(2)}, u32[]{:S(2)}) %collective-permute-start) | collective-permute-done | bytes 131104 | tf_op jit(solution)/shard_map/while/body/eval_jaxpr/ppermute | solution.py:19
  279.5 2.1 fusion.114
  284.4 6.6 %collective-permute-done = bf16[256,256]{0,1:T(8,128)(2,1)S(1)} collective-permute-done((bf16[256,256]{0,1:T(8,128)(2,1)S(1)}, bf16[256,256]{0,1:T(8,128)(2,1)S(1)}, u32[]{:S(2)}, u32[]{:S(2)}) %collective-permute-start) | collective-permute-done | bytes 131104 | tf_op jit(solution)/shard_map/while/body/eval_jaxpr/ppermute | solution.py:19
  298.2 2.1 fusion.114
  303.1 6.6 %collective-permute-done = bf16[256,256]{0,1:T(8,128)(2,1)S(1)} collective-permute-done((bf16[256,256]{0,1:T(8,128)(2,1)S(1)}, bf16[256,256]{0,1:T(8,128)(2,1)S(1)}, u32[]{:S(2)}, u32[]{:S(2)}) %collective-permute-start) | collective-permute-done | bytes 131104 | tf_op jit(solution)/shard_map/while/body/eval_jaxpr/ppermute | solution.py:19
  316.8 2.1 fusion.114
  322.5 4.6 convolution_convert_fusion
  328.9 16.3 %reduce-scatter.2.cloned.1.call-done = bf16[256,1024]{1,0:T(8,128)(2,1)} async-done(((bf16[256,2048]{1,0:T(8,128)(2,1)}), bf16[256,1024]{1,0:T(8,128)(2,1)}) %reduce-scatter.2.cloned.1.call-update) | async-done | bytes 524304 | tf_op jit(solution)/shard_map/reduce_scatter | solution.py:172
  347.8 78.9 %all-gather.2.cloned.1.call-done = f32[32,32,2048]{2,1,0:T(8,128)} async-done(((f32[1,32,2048]{2,1,0:T(8,128)}), f32[32,32,2048]{2,1,0:T(8,128)}) %all-gather.2.cloned.1.call-update) | async-done | bytes 8388624 | tf_op jit(solution)/shard_map/all_gather | solution.py:185
  426.6 3.8 reduce_sum.120
  430.7 3.6 convolution_reduce_fusion
  435.1 39.2 %pmax.7 = f32[32]{0:T(128)} all-reduce(f32[32]{0:T(128)S(1)} %convolution_reduce_fusion), channel_id=1, replica_groups=mesh['seq'=16,'mp'=2] {'seq','mp'}, use_global_device_ids=true, to_apply=%region_19.20 | all-reduce | flops 32 | bytes 256 | tf_op jit(solution)/shard_map/pmax | solution.py:189
  (454 shorter events, 163.3 us)
Async XLA Ops:
  7.2 6.4 %copy-start.30 = (s32[32]{0:T(128)S(1)}, s32[32]{0:T(128)}, u32[]{:S(2)}) copy-start(s32[32]{0:T(128)} %param.12) | copy-start | bytes 388
  7.2 338.0 %reduce-scatter.2.cloned.1.call-start = ((), (), s32[]{:S(2)}) async-start(), calls=%async_computation.1 | async-start | bytes 1572864 | tf_op jit(solution)/shard_map/reduce_scatter | solution.py:172
  10.0 10.1 %copy-start.1 = (bf16[256,2048]{1,0:T(8,128)(2,1)S(1)}, bf16[256,2048]{1,0:T(8,128)(2,1)}, u32[]{:S(2)}) copy-start(bf16[256,2048]{1,0:T(8,128)(2,1)} %param.11) | copy-start | bytes 3145732
  12.9 11.3 %copy-start.6 = (bf16[256,256]{1,0:T(8,128)(2,1)}, bf16[256,256]{1,0:T(8,128)(2,1)S(1)}, u32[]{:S(2)}) copy-start(bf16[256,256]{1,0:T(8,128)(2,1)S(1)} %slice.98) | copy-start | bytes 393220
  17.9 7.2 %copy-start.8 = (bf16[256,256]{1,0:T(8,128)(2,1)}, bf16[256,256]{1,0:T(8,128)(2,1)S(1)}, u32[]{:S(2)}) copy-start(bf16[256,256]{1,0:T(8,128)(2,1)S(1)} %copy.57) | copy-start | bytes 393220
  20.1 4.1 copy-start.13
  20.1 4.1 copy-start.15
  20.1 4.9 %copy-start.20 = (s32[256]{0:T(256)S(1)}, s32[256]{0:T(256)}, u32[]{:S(2)}) copy-start(s32[256]{0:T(256)} %copy-done.19) | copy-start | bytes 3076
  20.1 4.9 %copy-start.27 = (s32[256]{0:T(256)S(1)}, s32[256]{0:T(256)}, u32[]{:S(2)}) copy-start(s32[256]{0:T(256)} %copy-done.26) | copy-start | bytes 3076
  24.2 3.5 copy-start.11
  40.4 8.1 %collective-permute-start = (bf16[256,256]{0,1:T(8,128)(2,1)S(1)}, bf16[256,256]{0,1:T(8,128)(2,1)S(1)}, u32[]{:S(2)}, u32[]{:S(2)}) collective-permute-start(bf16[256,256]{0,1:T(8,128)(2,1)S(1)} %get-tuple-element.568), channel_id=1, source_target_pairs={{30,0},{0,2},{2,4},{4,6},{6,8},{8,10},{10,12},{12,14},{14,16},{16,... | collective-permute-start | bytes 393224 | tf_op jit(solution)/shard_map/while/body/eval_jaxpr/ppermute | solution.py:19
  40.9 10.4 %collective-permute-start.1 = (bf16[4,128,256]{1,0,2:T(4,128)(2,1)S(1)}, bf16[4,128,256]{1,0,2:T(4,128)(2,1)S(1)}, u32[]{:S(2)}, u32[]{:S(2)}) collective-permute-start(bf16[4,128,256]{1,0,2:T(4,128)(2,1)S(1)} %get-tuple-element.567), channel_id=1, source_target_pairs={{30,0},{0,2},{2,4},{4,6},{6,8},{8,10},{10,12},{12,14},{14,16},{16,... | collective-permute-start | bytes 786440 | tf_op jit(solution)/shard_map/while/body/eval_jaxpr/ppermute | solution.py:19
  60.0 7.1 %collective-permute-start = (bf16[256,256]{0,1:T(8,128)(2,1)S(1)}, bf16[256,256]{0,1:T(8,128)(2,1)S(1)}, u32[]{:S(2)}, u32[]{:S(2)}) collective-permute-start(bf16[256,256]{0,1:T(8,128)(2,1)S(1)} %get-tuple-element.568), channel_id=1, source_target_pairs={{30,0},{0,2},{2,4},{4,6},{6,8},{8,10},{10,12},{12,14},{14,16},{16,... | collective-permute-start | bytes 393224 | tf_op jit(solution)/shard_map/while/body/eval_jaxpr/ppermute | solution.py:19
  60.1 9.9 %collective-permute-start.1 = (bf16[4,128,256]{1,0,2:T(4,128)(2,1)S(1)}, bf16[4,128,256]{1,0,2:T(4,128)(2,1)S(1)}, u32[]{:S(2)}, u32[]{:S(2)}) collective-permute-start(bf16[4,128,256]{1,0,2:T(4,128)(2,1)S(1)} %get-tuple-element.567), channel_id=1, source_target_pairs={{30,0},{0,2},{2,4},{4,6},{6,8},{8,10},{10,12},{12,14},{14,16},{16,... | collective-permute-start | bytes 786440 | tf_op jit(solution)/shard_map/while/body/eval_jaxpr/ppermute | solution.py:19
  78.7 7.1 %collective-permute-start = (bf16[256,256]{0,1:T(8,128)(2,1)S(1)}, bf16[256,256]{0,1:T(8,128)(2,1)S(1)}, u32[]{:S(2)}, u32[]{:S(2)}) collective-permute-start(bf16[256,256]{0,1:T(8,128)(2,1)S(1)} %get-tuple-element.568), channel_id=1, source_target_pairs={{30,0},{0,2},{2,4},{4,6},{6,8},{8,10},{10,12},{12,14},{14,16},{16,... | collective-permute-start | bytes 393224 | tf_op jit(solution)/shard_map/while/body/eval_jaxpr/ppermute | solution.py:19
  78.7 9.9 %collective-permute-start.1 = (bf16[4,128,256]{1,0,2:T(4,128)(2,1)S(1)}, bf16[4,128,256]{1,0,2:T(4,128)(2,1)S(1)}, u32[]{:S(2)}, u32[]{:S(2)}) collective-permute-start(bf16[4,128,256]{1,0,2:T(4,128)(2,1)S(1)} %get-tuple-element.567), channel_id=1, source_target_pairs={{30,0},{0,2},{2,4},{4,6},{6,8},{8,10},{10,12},{12,14},{14,16},{16,... | collective-permute-start | bytes 786440 | tf_op jit(solution)/shard_map/while/body/eval_jaxpr/ppermute | solution.py:19
  97.3 7.1 %collective-permute-start = (bf16[256,256]{0,1:T(8,128)(2,1)S(1)}, bf16[256,256]{0,1:T(8,128)(2,1)S(1)}, u32[]{:S(2)}, u32[]{:S(2)}) collective-permute-start(bf16[256,256]{0,1:T(8,128)(2,1)S(1)} %get-tuple-element.568), channel_id=1, source_target_pairs={{30,0},{0,2},{2,4},{4,6},{6,8},{8,10},{10,12},{12,14},{14,16},{16,... | collective-permute-start | bytes 393224 | tf_op jit(solution)/shard_map/while/body/eval_jaxpr/ppermute | solution.py:19
  97.4 9.9 %collective-permute-start.1 = (bf16[4,128,256]{1,0,2:T(4,128)(2,1)S(1)}, bf16[4,128,256]{1,0,2:T(4,128)(2,1)S(1)}, u32[]{:S(2)}, u32[]{:S(2)}) collective-permute-start(bf16[4,128,256]{1,0,2:T(4,128)(2,1)S(1)} %get-tuple-element.567), channel_id=1, source_target_pairs={{30,0},{0,2},{2,4},{4,6},{6,8},{8,10},{10,12},{12,14},{14,16},{16,... | collective-permute-start | bytes 786440 | tf_op jit(solution)/shard_map/while/body/eval_jaxpr/ppermute | solution.py:19
  116.0 7.1 %collective-permute-start = (bf16[256,256]{0,1:T(8,128)(2,1)S(1)}, bf16[256,256]{0,1:T(8,128)(2,1)S(1)}, u32[]{:S(2)}, u32[]{:S(2)}) collective-permute-start(bf16[256,256]{0,1:T(8,128)(2,1)S(1)} %get-tuple-element.568), channel_id=1, source_target_pairs={{30,0},{0,2},{2,4},{4,6},{6,8},{8,10},{10,12},{12,14},{14,16},{16,... | collective-permute-start | bytes 393224 | tf_op jit(solution)/shard_map/while/body/eval_jaxpr/ppermute | solution.py:19
  116.1 9.9 %collective-permute-start.1 = (bf16[4,128,256]{1,0,2:T(4,128)(2,1)S(1)}, bf16[4,128,256]{1,0,2:T(4,128)(2,1)S(1)}, u32[]{:S(2)}, u32[]{:S(2)}) collective-permute-start(bf16[4,128,256]{1,0,2:T(4,128)(2,1)S(1)} %get-tuple-element.567), channel_id=1, source_target_pairs={{30,0},{0,2},{2,4},{4,6},{6,8},{8,10},{10,12},{12,14},{14,16},{16,... | collective-permute-start | bytes 786440 | tf_op jit(solution)/shard_map/while/body/eval_jaxpr/ppermute | solution.py:19
  134.6 7.1 %collective-permute-start = (bf16[256,256]{0,1:T(8,128)(2,1)S(1)}, bf16[256,256]{0,1:T(8,128)(2,1)S(1)}, u32[]{:S(2)}, u32[]{:S(2)}) collective-permute-start(bf16[256,256]{0,1:T(8,128)(2,1)S(1)} %get-tuple-element.568), channel_id=1, source_target_pairs={{30,0},{0,2},{2,4},{4,6},{6,8},{8,10},{10,12},{12,14},{14,16},{16,... | collective-permute-start | bytes 393224 | tf_op jit(solution)/shard_map/while/body/eval_jaxpr/ppermute | solution.py:19
  134.7 9.9 %collective-permute-start.1 = (bf16[4,128,256]{1,0,2:T(4,128)(2,1)S(1)}, bf16[4,128,256]{1,0,2:T(4,128)(2,1)S(1)}, u32[]{:S(2)}, u32[]{:S(2)}) collective-permute-start(bf16[4,128,256]{1,0,2:T(4,128)(2,1)S(1)} %get-tuple-element.567), channel_id=1, source_target_pairs={{30,0},{0,2},{2,4},{4,6},{6,8},{8,10},{10,12},{12,14},{14,16},{16,... | collective-permute-start | bytes 786440 | tf_op jit(solution)/shard_map/while/body/eval_jaxpr/ppermute | solution.py:19
  153.3 7.1 %collective-permute-start = (bf16[256,256]{0,1:T(8,128)(2,1)S(1)}, bf16[256,256]{0,1:T(8,128)(2,1)S(1)}, u32[]{:S(2)}, u32[]{:S(2)}) collective-permute-start(bf16[256,256]{0,1:T(8,128)(2,1)S(1)} %get-tuple-element.568), channel_id=1, source_target_pairs={{30,0},{0,2},{2,4},{4,6},{6,8},{8,10},{10,12},{12,14},{14,16},{16,... | collective-permute-start | bytes 393224 | tf_op jit(solution)/shard_map/while/body/eval_jaxpr/ppermute | solution.py:19
  153.4 9.9 %collective-permute-start.1 = (bf16[4,128,256]{1,0,2:T(4,128)(2,1)S(1)}, bf16[4,128,256]{1,0,2:T(4,128)(2,1)S(1)}, u32[]{:S(2)}, u32[]{:S(2)}) collective-permute-start(bf16[4,128,256]{1,0,2:T(4,128)(2,1)S(1)} %get-tuple-element.567), channel_id=1, source_target_pairs={{30,0},{0,2},{2,4},{4,6},{6,8},{8,10},{10,12},{12,14},{14,16},{16,... | collective-permute-start | bytes 786440 | tf_op jit(solution)/shard_map/while/body/eval_jaxpr/ppermute | solution.py:19
  171.9 7.1 %collective-permute-start = (bf16[256,256]{0,1:T(8,128)(2,1)S(1)}, bf16[256,256]{0,1:T(8,128)(2,1)S(1)}, u32[]{:S(2)}, u32[]{:S(2)}) collective-permute-start(bf16[256,256]{0,1:T(8,128)(2,1)S(1)} %get-tuple-element.568), channel_id=1, source_target_pairs={{30,0},{0,2},{2,4},{4,6},{6,8},{8,10},{10,12},{12,14},{14,16},{16,... | collective-permute-start | bytes 393224 | tf_op jit(solution)/shard_map/while/body/eval_jaxpr/ppermute | solution.py:19
  172.0 9.9 %collective-permute-start.1 = (bf16[4,128,256]{1,0,2:T(4,128)(2,1)S(1)}, bf16[4,128,256]{1,0,2:T(4,128)(2,1)S(1)}, u32[]{:S(2)}, u32[]{:S(2)}) collective-permute-start(bf16[4,128,256]{1,0,2:T(4,128)(2,1)S(1)} %get-tuple-element.567), channel_id=1, source_target_pairs={{30,0},{0,2},{2,4},{4,6},{6,8},{8,10},{10,12},{12,14},{14,16},{16,... | collective-permute-start | bytes 786440 | tf_op jit(solution)/shard_map/while/body/eval_jaxpr/ppermute | solution.py:19
  190.6 7.1 %collective-permute-start = (bf16[256,256]{0,1:T(8,128)(2,1)S(1)}, bf16[256,256]{0,1:T(8,128)(2,1)S(1)}, u32[]{:S(2)}, u32[]{:S(2)}) collective-permute-start(bf16[256,256]{0,1:T(8,128)(2,1)S(1)} %get-tuple-element.568), channel_id=1, source_target_pairs={{30,0},{0,2},{2,4},{4,6},{6,8},{8,10},{10,12},{12,14},{14,16},{16,... | collective-permute-start | bytes 393224 | tf_op jit(solution)/shard_map/while/body/eval_jaxpr/ppermute | solution.py:19
  190.7 9.9 %collective-permute-start.1 = (bf16[4,128,256]{1,0,2:T(4,128)(2,1)S(1)}, bf16[4,128,256]{1,0,2:T(4,128)(2,1)S(1)}, u32[]{:S(2)}, u32[]{:S(2)}) collective-permute-start(bf16[4,128,256]{1,0,2:T(4,128)(2,1)S(1)} %get-tuple-element.567), channel_id=1, source_target_pairs={{30,0},{0,2},{2,4},{4,6},{6,8},{8,10},{10,12},{12,14},{14,16},{16,... | collective-permute-start | bytes 786440 | tf_op jit(solution)/shard_map/while/body/eval_jaxpr/ppermute | solution.py:19
  209.2 7.1 %collective-permute-start = (bf16[256,256]{0,1:T(8,128)(2,1)S(1)}, bf16[256,256]{0,1:T(8,128)(2,1)S(1)}, u32[]{:S(2)}, u32[]{:S(2)}) collective-permute-start(bf16[256,256]{0,1:T(8,128)(2,1)S(1)} %get-tuple-element.568), channel_id=1, source_target_pairs={{30,0},{0,2},{2,4},{4,6},{6,8},{8,10},{10,12},{12,14},{14,16},{16,... | collective-permute-start | bytes 393224 | tf_op jit(solution)/shard_map/while/body/eval_jaxpr/ppermute | solution.py:19
  209.3 9.9 %collective-permute-start.1 = (bf16[4,128,256]{1,0,2:T(4,128)(2,1)S(1)}, bf16[4,128,256]{1,0,2:T(4,128)(2,1)S(1)}, u32[]{:S(2)}, u32[]{:S(2)}) collective-permute-start(bf16[4,128,256]{1,0,2:T(4,128)(2,1)S(1)} %get-tuple-element.567), channel_id=1, source_target_pairs={{30,0},{0,2},{2,4},{4,6},{6,8},{8,10},{10,12},{12,14},{14,16},{16,... | collective-permute-start | bytes 786440 | tf_op jit(solution)/shard_map/while/body/eval_jaxpr/ppermute | solution.py:19
  227.9 7.1 %collective-permute-start = (bf16[256,256]{0,1:T(8,128)(2,1)S(1)}, bf16[256,256]{0,1:T(8,128)(2,1)S(1)}, u32[]{:S(2)}, u32[]{:S(2)}) collective-permute-start(bf16[256,256]{0,1:T(8,128)(2,1)S(1)} %get-tuple-element.568), channel_id=1, source_target_pairs={{30,0},{0,2},{2,4},{4,6},{6,8},{8,10},{10,12},{12,14},{14,16},{16,... | collective-permute-start | bytes 393224 | tf_op jit(solution)/shard_map/while/body/eval_jaxpr/ppermute | solution.py:19
  228.0 9.9 %collective-permute-start.1 = (bf16[4,128,256]{1,0,2:T(4,128)(2,1)S(1)}, bf16[4,128,256]{1,0,2:T(4,128)(2,1)S(1)}, u32[]{:S(2)}, u32[]{:S(2)}) collective-permute-start(bf16[4,128,256]{1,0,2:T(4,128)(2,1)S(1)} %get-tuple-element.567), channel_id=1, source_target_pairs={{30,0},{0,2},{2,4},{4,6},{6,8},{8,10},{10,12},{12,14},{14,16},{16,... | collective-permute-start | bytes 786440 | tf_op jit(solution)/shard_map/while/body/eval_jaxpr/ppermute | solution.py:19
  246.6 7.1 %collective-permute-start = (bf16[256,256]{0,1:T(8,128)(2,1)S(1)}, bf16[256,256]{0,1:T(8,128)(2,1)S(1)}, u32[]{:S(2)}, u32[]{:S(2)}) collective-permute-start(bf16[256,256]{0,1:T(8,128)(2,1)S(1)} %get-tuple-element.568), channel_id=1, source_target_pairs={{30,0},{0,2},{2,4},{4,6},{6,8},{8,10},{10,12},{12,14},{14,16},{16,... | collective-permute-start | bytes 393224 | tf_op jit(solution)/shard_map/while/body/eval_jaxpr/ppermute | solution.py:19
  246.6 9.9 %collective-permute-start.1 = (bf16[4,128,256]{1,0,2:T(4,128)(2,1)S(1)}, bf16[4,128,256]{1,0,2:T(4,128)(2,1)S(1)}, u32[]{:S(2)}, u32[]{:S(2)}) collective-permute-start(bf16[4,128,256]{1,0,2:T(4,128)(2,1)S(1)} %get-tuple-element.567), channel_id=1, source_target_pairs={{30,0},{0,2},{2,4},{4,6},{6,8},{8,10},{10,12},{12,14},{14,16},{16,... | collective-permute-start | bytes 786440 | tf_op jit(solution)/shard_map/while/body/eval_jaxpr/ppermute | solution.py:19
  265.2 7.1 %collective-permute-start = (bf16[256,256]{0,1:T(8,128)(2,1)S(1)}, bf16[256,256]{0,1:T(8,128)(2,1)S(1)}, u32[]{:S(2)}, u32[]{:S(2)}) collective-permute-start(bf16[256,256]{0,1:T(8,128)(2,1)S(1)} %get-tuple-element.568), channel_id=1, source_target_pairs={{30,0},{0,2},{2,4},{4,6},{6,8},{8,10},{10,12},{12,14},{14,16},{16,... | collective-permute-start | bytes 393224 | tf_op jit(solution)/shard_map/while/body/eval_jaxpr/ppermute | solution.py:19
  265.3 9.9 %collective-permute-start.1 = (bf16[4,128,256]{1,0,2:T(4,128)(2,1)S(1)}, bf16[4,128,256]{1,0,2:T(4,128)(2,1)S(1)}, u32[]{:S(2)}, u32[]{:S(2)}) collective-permute-start(bf16[4,128,256]{1,0,2:T(4,128)(2,1)S(1)} %get-tuple-element.567), channel_id=1, source_target_pairs={{30,0},{0,2},{2,4},{4,6},{6,8},{8,10},{10,12},{12,14},{14,16},{16,... | collective-permute-start | bytes 786440 | tf_op jit(solution)/shard_map/while/body/eval_jaxpr/ppermute | solution.py:19
  283.9 7.1 %collective-permute-start = (bf16[256,256]{0,1:T(8,128)(2,1)S(1)}, bf16[256,256]{0,1:T(8,128)(2,1)S(1)}, u32[]{:S(2)}, u32[]{:S(2)}) collective-permute-start(bf16[256,256]{0,1:T(8,128)(2,1)S(1)} %get-tuple-element.568), channel_id=1, source_target_pairs={{30,0},{0,2},{2,4},{4,6},{6,8},{8,10},{10,12},{12,14},{14,16},{16,... | collective-permute-start | bytes 393224 | tf_op jit(solution)/shard_map/while/body/eval_jaxpr/ppermute | solution.py:19
  283.9 9.9 %collective-permute-start.1 = (bf16[4,128,256]{1,0,2:T(4,128)(2,1)S(1)}, bf16[4,128,256]{1,0,2:T(4,128)(2,1)S(1)}, u32[]{:S(2)}, u32[]{:S(2)}) collective-permute-start(bf16[4,128,256]{1,0,2:T(4,128)(2,1)S(1)} %get-tuple-element.567), channel_id=1, source_target_pairs={{30,0},{0,2},{2,4},{4,6},{6,8},{8,10},{10,12},{12,14},{14,16},{16,... | collective-permute-start | bytes 786440 | tf_op jit(solution)/shard_map/while/body/eval_jaxpr/ppermute | solution.py:19
  302.5 7.1 %collective-permute-start = (bf16[256,256]{0,1:T(8,128)(2,1)S(1)}, bf16[256,256]{0,1:T(8,128)(2,1)S(1)}, u32[]{:S(2)}, u32[]{:S(2)}) collective-permute-start(bf16[256,256]{0,1:T(8,128)(2,1)S(1)} %get-tuple-element.568), channel_id=1, source_target_pairs={{30,0},{0,2},{2,4},{4,6},{6,8},{8,10},{10,12},{12,14},{14,16},{16,... | collective-permute-start | bytes 393224 | tf_op jit(solution)/shard_map/while/body/eval_jaxpr/ppermute | solution.py:19
  302.6 9.9 %collective-permute-start.1 = (bf16[4,128,256]{1,0,2:T(4,128)(2,1)S(1)}, bf16[4,128,256]{1,0,2:T(4,128)(2,1)S(1)}, u32[]{:S(2)}, u32[]{:S(2)}) collective-permute-start(bf16[4,128,256]{1,0,2:T(4,128)(2,1)S(1)} %get-tuple-element.567), channel_id=1, source_target_pairs={{30,0},{0,2},{2,4},{4,6},{6,8},{8,10},{10,12},{12,14},{14,16},{16,... | collective-permute-start | bytes 786440 | tf_op jit(solution)/shard_map/while/body/eval_jaxpr/ppermute | solution.py:19
  322.5 4.9 %copy-start.2 = (bf16[256,2048]{1,0:T(8,128)(2,1)S(1)}, bf16[256,2048]{1,0:T(8,128)(2,1)}, u32[]{:S(2)}) copy-start(bf16[256,2048]{1,0:T(8,128)(2,1)} %param.11) | copy-start | bytes 3145732
  327.1 19.7 %copy-start.29 = (s32[32]{0:T(128)S(1)}, s32[32]{0:T(128)}, u32[]{:S(2)}) copy-start(s32[32]{0:T(128)} %get-tuple-element.432) | copy-start | bytes 388
  327.1 20.7 %copy-start.28 = (bf16[2048]{0:T(1024)(128)(2,1)S(1)}, bf16[2048]{0:T(1024)(128)(2,1)}, u32[]{:S(2)}) copy-start(bf16[2048]{0:T(1024)(128)(2,1)} %param.18) | copy-start | bytes 12292
  327.1 99.6 %all-gather.2.cloned.1.call-start = ((), (), s32[]{:S(2)}) async-start(), calls=%async_computation.2 | async-start | bytes 8650752 | tf_op jit(solution)/shard_map/all_gather | solution.py:185
  346.7 83.7 %copy-start.4 = (bf16[256,1024]{1,0:T(8,128)(2,1)}, bf16[256,1024]{1,0:T(8,128)(2,1)S(1)}, u32[]{:S(2)}) copy-start(bf16[256,1024]{1,0:T(8,128)(2,1)S(1)} %add_convert_fusion) | copy-start | bytes 1572868
  430.5 3.9 copy-start.7
  430.5 3.9 copy-start.9
  430.7 43.5 %copy-start.10 = (bf16[32,2048]{1,0:T(8,128)(2,1)}, bf16[32,2048]{1,0:T(8,128)(2,1)S(1)}, u32[]{:S(2)}) copy-start(bf16[32,2048]{1,0:T(8,128)(2,1)S(1)} %multiply_convert_fusion.3) | copy-start | bytes 393220
  (29 other events, 40.9 us)
Sparse Core Ops, SparseCore 0:
  327.2 17.9 reduce-scatter.1
  349.2 77.3 all-gather.1
